TPU v7x, 32 devices: a whole 2x2x4 slice. The times are simulated.
32 devices in a mesh: group: 2 (over y), seq: 8 (over z, x), chan: 2 (over core).
Axes of the slice: x: 2, y: 2, z: 4, core: 2. Of those that a mesh axis runs over, the one named last changes fastest.
Arguments:
- fresh: bfloat16 [2048, 3, 2048], P(('group', 'seq'), None, 'chan'), parts along dimension 0, may hold values from -6 to 6
- library: bfloat16 [8, 8, 2048], P('seq', None, 'chan'), may hold values from -6 to 6
- block_slot: int32 [8], replicated, may hold values from 0 to 7, each once
- prefix_blocks: int32 [16, 4], P('group'), parts along dimension 0, may hold values from 0 to 7, all different within a row
- short_taps: float32 [3, 3, 2048], P(None, None, 'chan'), may hold values from -4 to 4
- long_filter: float32 [1024, 2048], P('seq', 'chan'), may hold values from -2 to 2
- skip_gain: float32 [2048], P('chan'), may hold values from -6 to 6
Outputs:
- mixed: bfloat16 [2048, 2048], P(('group', 'seq'), 'chan'), parts along dimension 0
There are 2 independent parts, one for each index of `group`. A program takes and returns all parts, laid end to end along the dimension named above; an argument that names none is the same for every part. Nothing has to cross between parts.
Inputs may be any that keep to these rules, and one draw needn't show every extreme that they name: `block_slot`: each number appears once. `prefix_blocks`: every library block is named at least once; the four entries of a row differ.
All inputs are finite; a program needn't handle non-finite values.
Results may differ from a plain program's by a relative error of at most 0.008.
Values may be sent and summed in bfloat16 or wider, within the bound.
No kernel may reach another device: no remote copies, remote signals or barrier semaphores. Data moves between devices by JAX's collectives and lax.ppermute only.
A program may use at most 64 MiB of HBM per device.

v0:
```python
import math

import jax
import jax.numpy as jnp
from jax import lax
from jax.sharding import PartitionSpec as P

TAPS = 3
BLK = 8


def from_behind(shard, axis, by):
    count = lax.axis_size(axis)
    pairs = [(i, i + by) for i in range(count) if 0 <= i + by < count]
    return lax.ppermute(shard, axis, pairs)


def exact_dot(pattern, matrix, tensor):
    return jnp.einsum(pattern, matrix, tensor, precision=lax.Precision.HIGHEST)


def turn_angles(numbers, period):
    return (numbers % period).astype(jnp.float32) * (2.0 * math.pi / period)


def body(fresh, library, block_slot, prefix_blocks, short_taps, long_filter, skip_gain):
    row_count = fresh.shape[0]
    channels = fresh.shape[2]
    devices = lax.axis_size("seq")
    seq_index = lax.axis_index("seq")
    group_rows = row_count // devices
    period = 2 * row_count * devices
    block_ids = jnp.arange(devices, dtype=jnp.int32)
    mode_ids = jnp.arange(2 * devices, dtype=jnp.int32)
    coarse = turn_angles(mode_ids[:, None] * block_ids[None, :], 2 * devices)
    cos_q = jnp.cos(coarse)
    sin_q = jnp.sin(coarse)
    local_rows = seq_index * group_rows + jnp.arange(group_rows, dtype=jnp.int32)
    twist = turn_angles(mode_ids[:, None] * local_rows[None, :], period)
    twist_cos = jnp.cos(twist)[:, :, None]
    twist_sin = jnp.sin(twist)[:, :, None]
    row_ids = jnp.arange(row_count, dtype=jnp.int32)
    fine_angles = turn_angles(row_ids[:, None] * row_ids[None, :], row_count)
    cos_m = jnp.cos(fine_angles)
    sin_m = jnp.sin(fine_angles)
    first_modes = 2 * seq_index + jnp.arange(2, dtype=jnp.int32)
    back_twist = turn_angles(first_modes[:, None] * row_ids[None, :], period)
    back_cos = jnp.cos(back_twist)[:, :, None]
    back_sin = jnp.sin(back_twist)[:, :, None]

    def to_modes(column):
        real_part = exact_dot("kq,qgc->kgc", cos_q, column)
        imag_part = -exact_dot("kq,qgc->kgc", sin_q, column)
        return jnp.stack(
            [
                real_part * twist_cos + imag_part * twist_sin,
                imag_part * twist_cos - real_part * twist_sin,
            ]
        )

    def to_spectrum(spread):
        real_part = exact_dot("ki,jic->jkc", cos_m, spread[0]) + exact_dot(
            "ki,jic->jkc", sin_m, spread[1]
        )
        imag_part = exact_dot("ki,jic->jkc", cos_m, spread[1]) - exact_dot(
            "ki,jic->jkc", sin_m, spread[0]
        )
        return (real_part, imag_part)

    blocks_here = row_count // BLK
    flat_ids = prefix_blocks.reshape(-1)
    first_block = jnp.minimum(seq_index * blocks_here, flat_ids.shape[0] - blocks_here)
    own_ids = lax.dynamic_slice_in_dim(flat_ids, first_block, blocks_here)
    matches = own_ids[:, None] == jnp.arange(block_slot.shape[0], dtype=jnp.int32)[None, :]
    wanted = jnp.sum(jnp.where(matches, block_slot[None, :], 0), axis=1)
    shards = lax.all_gather(library, "seq", axis=0, tiled=True)
    picker = (wanted[:, None] == jnp.arange(shards.shape[0], dtype=jnp.int32)[None, :]).astype(
        jnp.bfloat16
    )
    gathered = jnp.einsum("bn,nlc->blc", picker, shards, preferred_element_type=jnp.float32)
    cached = gathered.reshape(row_count, channels).astype(jnp.bfloat16)
    values = jnp.where(seq_index < devices // 4, cached, fresh[:, 2])
    stacked = jnp.concatenate([fresh[:, :2], values[:, None]], axis=1)
    previous = from_behind(stacked[row_count - (TAPS - 1) :], "seq", 1)
    extended = jnp.concatenate([previous, stacked], axis=0)
    shortened = jnp.zeros((row_count, 3, channels), jnp.float32)
    for offset in range(TAPS):
        window_start = TAPS - 1 - offset
        shortened = shortened + short_taps[offset][None] * extended[
            window_start : window_start + row_count
        ].astype(jnp.float32)
    gating = shortened[:, 0]
    signal = shortened[:, 1] * shortened[:, 2]
    spread_signal = to_modes(
        lax.all_to_all(signal[None], "seq", split_axis=1, concat_axis=0, tiled=True)
    )
    spread_taps = to_modes(
        lax.all_to_all(long_filter[None], "seq", split_axis=1, concat_axis=0, tiled=True)
    )
    moved_signal, moved_taps = (
        lax.all_to_all(
            spread_signal.astype(jnp.bfloat16), "seq", split_axis=1, concat_axis=2, tiled=True
        ).astype(spread_signal.dtype),
        lax.all_to_all(
            spread_taps.astype(jnp.bfloat16), "seq", split_axis=1, concat_axis=2, tiled=True
        ).astype(spread_taps.dtype),
    )
    sig_real, sig_imag = to_spectrum(moved_signal)
    tap_real, tap_imag = to_spectrum(moved_taps)
    prod_real = sig_real * tap_real - sig_imag * tap_imag
    prod_imag = sig_real * tap_imag + sig_imag * tap_real
    back_real = exact_dot("ki,jic->jkc", cos_m, prod_real) - exact_dot(
        "ki,jic->jkc", sin_m, prod_imag
    )
    back_imag = exact_dot("ki,jic->jkc", cos_m, prod_imag) + exact_dot(
        "ki,jic->jkc", sin_m, prod_real
    )
    turned = jnp.stack(
        [back_real * back_cos - back_imag * back_sin, back_imag * back_cos + back_real * back_sin]
    )
    spread = lax.all_to_all(turned, "seq", split_axis=2, concat_axis=1, tiled=True)
    positions = (
        exact_dot("kq,kgc->qgc", cos_q, spread[0]) - exact_dot("kq,kgc->qgc", sin_q, spread[1])
    ) / period
    convolved = lax.all_to_all(positions, "seq", split_axis=0, concat_axis=1, tiled=True)[0]
    output = gating * (convolved + skip_gain[None, :] * signal)
    return output.astype(jnp.bfloat16)


def solution(mesh):
    return jax.shard_map(
        body,
        mesh=mesh,
        in_specs=(
            P(("group", "seq"), None, "chan"),
            P("seq", None, "chan"),
            P(),
            P("group", None),
            P(None, None, "chan"),
            P("seq", "chan"),
            P("chan"),
        ),
        out_specs=P(("group", "seq"), "chan"),
        check_vma=False,
    )
```

profile of v0, /device:TPU:0, one launch (start us, length us, event | category | flops | bytes accessed | tf_op | source)
XLA Modules:
  0.0 217.2 jit_solution(2624598276856022187)
XLA Ops:
  0.0 2.3 %broadcast_in_dim.12 = f32[1,128,1024]{2,0,1:T(1,128)} reshape(f32[128,1024]{1,0:T(8,128)} %param.12) | data formatting | bytes 1048576 | tf_op jit(solution)/shard_map/broadcast_in_dim | solution.py:98
  2.3 7.3 %all-to-all-start.2 = ((f32[1,128,1024]{2,0,1:T(1,128)}), f32[1,128,1024]{2,0,1:T(1,128)S(1)}, u32[]{:S(2)}, u32[]{:S(2)}) async-start(f32[1,128,1024]{2,0,1:T(1,128)} %broadcast_in_dim.12), calls=%async_computation.2 | async-start | bytes 1048576 | tf_op jit(solution)/shard_map/all_to_all | solution.py:98
  9.8 37.2 %all_gather.3 = bf16[8,8,1024]{2,1,0:T(8,128)(2,1)S(1)} all-gather(bf16[1,8,1024]{2,1,0:T(8,128)(2,1)S(1)} %copy-done.7), channel_id=1, replica_groups=mesh['group'=2,'seq'=8,'chan'=2] {'seq'}, dimensions={0}, use_global_device_ids=true | all-gather | bytes 147456 | tf_op jit(solution)/shard_map/all_gather | solution.py:76
  52.4 5.6 %all-to-all-start = ((f32[1,128,1024]{2,0,1:T(1,128)}), f32[1,128,1024]{2,0,1:T(1,128)S(1)}, u32[]{:S(2)}, u32[]{:S(2)}) async-start(f32[1,128,1024]{2,0,1:T(1,128)} %copy.63), calls=%async_computation | async-start | bytes 1048576 | tf_op jit(solution)/shard_map/all_to_all | solution.py:95
  59.5 2.2 %fusion.15 = f32[16,16,1024]{2,0,1:T(8,128)} fusion(f32[8,16,1024]{2,1,0:T(8,128)S(1)} %bitcast.138), kind=kOutput, calls=%fused_computation.44 | convolution fusion | flops 25167616 | bytes 1572864 | tf_op jit(solution)/shard_map/kq,qgc->kgc/dot_general | solution.py:19
  61.7 6.6 %all-to-all-done = f32[1,128,1024]{2,0,1:T(1,128)S(1)} async-done(((f32[1,128,1024]{2,0,1:T(1,128)}), f32[1,128,1024]{2,0,1:T(1,128)S(1)}, u32[]{:S(2)}, u32[]{:S(2)}) %all-to-all-start) | async-done | bytes 524320 | tf_op jit(solution)/shard_map/all_to_all | solution.py:95
  69.7 2.5 %fusion.9 = (bf16[1,16,16,1024]{3,1,2,0:T(8,128)(2,1)S(1)}, bf16[1,16,16,1024]{3,1,2,0:T(8,128)(2,1)S(1)}, bf16[1,16,16,1024]{3,1,2,0:T(8,128)(2,1)S(1)}, bf16[1,16,16,1024]{3,1,2,0:T(8,128)(2,1)}) fusion(f32[16,16,1024]{2,0,1:T(8,128)S(1)} %convolution_negate_fusion, f32[16,16,1024]{2,0,1:T(8,128)S(1)} %copy-done.3, f32[16,16]{0,1:T(8,128)S(1)} %get-tuple-element.27, ...), kind=kOutput, calls=%fused_computation.35 | convolution fusion | flops 29361920 | bytes 5769216 | tf_op jit(solution)/shard_map/kq,qgc->kgc/dot_general | solution.py:19
  72.2 1.5 copy.74
  73.8 3.7 %all-to-all-start.3 = ((bf16[2,16,16,1024]{3,2,0,1:T(8,128)(2,1)}), bf16[2,16,16,1024]{3,2,0,1:T(8,128)(2,1)S(1)}, u32[]{:S(2)}, u32[]{:S(2)}) async-start(bf16[2,16,16,1024]{3,2,0,1:T(8,128)(2,1)} %copy.74), calls=%async_computation.3 | async-start | bytes 2097152 | tf_op jit(solution)/shard_map/all_to_all | solution.py:104
  78.6 1.6 copy.66
  80.2 14.4 %all-to-all-done.3 = bf16[2,16,16,1024]{3,2,0,1:T(8,128)(2,1)S(1)} async-done(((bf16[2,16,16,1024]{3,2,0,1:T(8,128)(2,1)}), bf16[2,16,16,1024]{3,2,0,1:T(8,128)(2,1)S(1)}, u32[]{:S(2)}, u32[]{:S(2)}) %all-to-all-start.3) | async-done | bytes 1048608 | tf_op jit(solution)/shard_map/all_to_all | solution.py:104
  95.6 3.7 %all-to-all-start.1 = ((bf16[2,16,16,1024]{3,2,0,1:T(8,128)(2,1)}), bf16[2,16,16,1024]{3,2,0,1:T(8,128)(2,1)S(1)}, u32[]{:S(2)}, u32[]{:S(2)}) async-start(bf16[2,16,16,1024]{3,2,0,1:T(8,128)(2,1)} %copy.66), calls=%async_computation.1 | async-start | bytes 2097152 | tf_op jit(solution)/shard_map/all_to_all | solution.py:101
  101.9 1.8 fusion.37
  103.7 1.9 convolution_subtract_fusion.1
  105.6 15.1 %all-to-all-done.1 = bf16[2,16,16,1024]{3,2,0,1:T(8,128)(2,1)S(1)} async-done(((bf16[2,16,16,1024]{3,2,0,1:T(8,128)(2,1)}), bf16[2,16,16,1024]{3,2,0,1:T(8,128)(2,1)S(1)}, u32[]{:S(2)}, u32[]{:S(2)}) %all-to-all-start.1) | async-done | bytes 1048608 | tf_op jit(solution)/shard_map/all_to_all | solution.py:101
  130.0 1.6 subtract_bitcast_fusion
  131.6 1.5 pad_maximum_fusion
  133.0 4.2 %copy.84 = f32[2,2,128,1024]{3,1,0,2:T(2,128)} copy(f32[2,2,128,1024]{2,3,1,0:T(8,128)} %pad_maximum_fusion) | data formatting | bytes 4194304 | tf_op jit(solution)/shard_map/stack | solution.py:118
  137.2 50.2 %all_to_all.78 = f32[2,2,128,1024]{3,1,0,2:T(2,128)S(1)} all-to-all(f32[2,2,128,1024]{3,1,0,2:T(2,128)} %copy.84), channel_id=1, replica_groups=mesh['group'=2,'seq'=8,'chan'=2] {'seq'}, dimensions={2} | all-to-all | bytes 4194304 | tf_op jit(solution)/shard_map/all_to_all | solution.py:121
  190.6 1.7 squeeze.36
  192.3 2.0 fusion.71
  194.3 1.8 copy.87
  196.1 1.9 squeeze.37
  199.0 17.3 %all_to_all.79 = f32[8,16,1024]{2,1,0:T(8,128)S(1)} all-to-all(f32[8,16,1024]{2,1,0:T(8,128)S(1)} %copy.88), channel_id=1, replica_groups=mesh['group'=2,'seq'=8,'chan'=2] {'seq'}, dimensions={0} | all-to-all | bytes 1048576 | tf_op jit(solution)/shard_map/all_to_all | solution.py:125
  (71 shorter events, 27.3 us)
Async XLA Ops:
  0.0 9.6 %copy-start.9 = (s32[8,4]{0,1:T(4,128)S(1)}, s32[8,4]{0,1:T(4,128)}, u32[]{:S(2)}) copy-start(s32[8,4]{0,1:T(4,128)} %param.10) | copy-start | bytes 388
  0.0 9.7 %copy-start.7 = (bf16[1,8,1024]{2,1,0:T(8,128)(2,1)S(1)}, bf16[1,8,1024]{2,1,0:T(8,128)(2,1)}, u32[]{:S(2)}) copy-start(bf16[1,8,1024]{2,1,0:T(8,128)(2,1)} %param.8) | copy-start | bytes 49156
  0.0 46.9 %copy-start.5 = (bf16[128,3,1024]{2,0,1:T(8,128)(2,1)S(1)}, bf16[128,3,1024]{2,0,1:T(8,128)(2,1)}, u32[]{:S(2)}) copy-start(bf16[128,3,1024]{2,0,1:T(8,128)(2,1)} %param.7) | copy-start | bytes 2359300
  0.0 47.1 %copy-start.10 = (s32[8]{0:T(128)S(1)}, s32[8]{0:T(128)}, u32[]{:S(2)}) copy-start(s32[8]{0:T(128)} %param.9) | copy-start | bytes 100
  2.3 50.1 %all-to-all-start.2 = ((f32[1,128,1024]{2,0,1:T(1,128)}), f32[1,128,1024]{2,0,1:T(1,128)S(1)}, u32[]{:S(2)}, u32[]{:S(2)}) async-start(f32[1,128,1024]{2,0,1:T(1,128)} %broadcast_in_dim.12), calls=%async_computation.2 | async-start | bytes 1048576 | tf_op jit(solution)/shard_map/all_to_all | solution.py:98
  9.7 39.2 %copy-start.6 = (f32[3,3,1024]{2,1,0:T(4,128)S(1)}, f32[3,3,1024]{2,1,0:T(4,128)}, u32[]{:S(2)}) copy-start(f32[3,3,1024]{2,1,0:T(4,128)} %param.11) | copy-start | bytes 110596
  47.6 2.7 %collective-permute-start = (bf16[2,3,1024]{2,0,1:T(2,128)(2,1)S(1)}, bf16[2,3,1024]{2,0,1:T(2,128)(2,1)S(1)}, u32[]{:S(2)}, u32[]{:S(2)}) collective-permute-start(bf16[2,3,1024]{2,0,1:T(2,128)(2,1)S(1)} %fusion.58), channel_id=1, source_target_pairs={{0,2},{2,4},{4,6},{6,8},{8,10},{10,12},{12,14},{1,3},{3,5},{5,7},{... | collective-permute-start | bytes 36872 | tf_op jit(solution)/shard_map/ppermute | solution.py:15
  52.4 15.9 %all-to-all-start = ((f32[1,128,1024]{2,0,1:T(1,128)}), f32[1,128,1024]{2,0,1:T(1,128)S(1)}, u32[]{:S(2)}, u32[]{:S(2)}) async-start(f32[1,128,1024]{2,0,1:T(1,128)} %copy.63), calls=%async_computation | async-start | bytes 1048576 | tf_op jit(solution)/shard_map/all_to_all | solution.py:95
  68.4 1.3 copy-start.3
  73.8 20.9 %all-to-all-start.3 = ((bf16[2,16,16,1024]{3,2,0,1:T(8,128)(2,1)}), bf16[2,16,16,1024]{3,2,0,1:T(8,128)(2,1)S(1)}, u32[]{:S(2)}, u32[]{:S(2)}) async-start(bf16[2,16,16,1024]{3,2,0,1:T(8,128)(2,1)} %copy.74), calls=%async_computation.3 | async-start | bytes 2097152 | tf_op jit(solution)/shard_map/all_to_all | solution.py:104
  94.6 1.0 copy-start
  95.6 25.0 %all-to-all-start.1 = ((bf16[2,16,16,1024]{3,2,0,1:T(8,128)(2,1)}), bf16[2,16,16,1024]{3,2,0,1:T(8,128)(2,1)S(1)}, u32[]{:S(2)}, u32[]{:S(2)}) async-start(bf16[2,16,16,1024]{3,2,0,1:T(8,128)(2,1)} %copy.66), calls=%async_computation.1 | async-start | bytes 2097152 | tf_op jit(solution)/shard_map/all_to_all | solution.py:101
  122.7 1.2 copy-start.1
  123.9 1.2 copy-start.2
  192.3 2.0 copy-start.4
  198.7 17.6 %copy-start.8 = (f32[1024]{0:T(1024)S(1)}, f32[1024]{0:T(1024)}, u32[]{:S(2)}) copy-start(f32[1024]{0:T(1024)} %param.13) | copy-start | bytes 12292
where the time goes:
time: 218 us; the launch traced here: 217 us
  blocking collectives  105 us (48%)
  waiting for transfers between devices  37.5 us (17%)
  matrix products  24.5 us (11%)
  local copies, waits for them, and re-layouts  23.8 us (11%)
  starting transfers between devices  21.6 us (10%)
  other arithmetic  4.82 us (2%)
    all_to_all x1, blocking collectives, body(): lax.all_to_all(turned, 'seq', split_axis=2, concat_axis=1, tiled=True)  50.2 us
    all_gather x1, blocking collectives, body(): shards = lax.all_gather(library, 'seq', axis=0, tiled=True)  37.2 us
    dot_general x18, matrix products, exact_dot(): return jnp.einsum(pattern, matrix, tensor, precision=lax.Precision.HIGHEST)  24.2 us
    all_to_all x1, blocking collectives, body(): lax.all_to_all(positions, 'seq', split_axis=0, concat_axis=1, tiled=True)[0]  17.3 us
    all_to_all x1, waiting for transfers between devices, body(): lax.all_to_all(spread_signal.astype(jnp.bfloat16), 'seq', split_axis=1, c...  15.1 us
    all_to_all x1, waiting for transfers between devices, body(): lax.all_to_all(spread_taps.astype(jnp.bfloat16), 'seq', split_axis=1, con...  14.4 us
    all_to_all x1, starting transfers between devices, body(): lax.all_to_all(long_filter[None], 'seq', split_axis=1, concat_axis=0, til...  7.29 us
    all_to_all x1, waiting for transfers between devices, body(): lax.all_to_all(signal[None], 'seq', split_axis=1, concat_axis=0, tiled=True)  6.61 us
  transfers between devices with their start and end apart: 5, of which 4 were waited for; matrix products, arithmetic and copies ran while one was open for 7% of the time, Pallas kernels for 0%

commit v1 on v0

--- a/solution.py
+++ b/solution.py
@@ -23,7 +23,7 @@
     return (numbers % period).astype(jnp.float32) * (2.0 * math.pi / period)
 
 
-def body(fresh, library, block_slot, prefix_blocks, short_taps, long_filter, skip_gain):
+def ring_body(fresh, library, block_slot, prefix_blocks, short_taps, long_filter, skip_gain):
     row_count = fresh.shape[0]
     channels = fresh.shape[2]
     devices = lax.axis_size("seq")
@@ -127,6 +127,85 @@
     return output.astype(jnp.bfloat16)
 
 
+def dft_tables(tokens):
+    period = 2 * tokens
+    width = 1
+    while width * width < tokens:
+        width *= 2
+    outer = tokens // width
+    freqs = jnp.arange(tokens + 1, dtype=jnp.int32)[:, None]
+    coarse = turn_angles(freqs * (width * jnp.arange(outer, dtype=jnp.int32))[None, :], period)
+    fine = turn_angles(freqs * jnp.arange(width, dtype=jnp.int32)[None, :], period)
+    c1, s1 = jnp.cos(coarse)[:, :, None], jnp.sin(coarse)[:, :, None]
+    c2, s2 = jnp.cos(fine)[:, None, :], jnp.sin(fine)[:, None, :]
+    cos_t = (c1 * c2 - s1 * s2).reshape(tokens + 1, tokens)
+    sin_t = (s1 * c2 + c1 * s2).reshape(tokens + 1, tokens)
+    return cos_t, sin_t
+
+
+def local_body(fresh, library, block_slot, prefix_blocks, short_taps, long_filter, skip_gain):
+    row_count, _, channels = fresh.shape
+    devices = lax.axis_size("seq")
+    seq_index = lax.axis_index("seq")
+    tokens = row_count * devices
+    own = channels // devices
+    lib_here = library.shape[0]
+    lib_rows = lib_here * BLK // 4
+    packed = jnp.concatenate([fresh, long_filter.astype(jnp.bfloat16)[:, None, :]], axis=1)
+    packed = jnp.concatenate([packed, library.reshape(lib_rows, 4, channels)], axis=0)
+    moved = lax.all_to_all(packed, "seq", split_axis=2, concat_axis=0, tiled=True)
+    moved = moved.reshape(devices, row_count + lib_rows, 4, own)
+    rows = moved[:, :row_count].reshape(tokens, 4, own)
+    lib_all = moved[:, row_count:].reshape(devices * lib_here, BLK * own)
+
+    slot_ids = block_slot[prefix_blocks.reshape(-1)]
+    prefix_len = slot_ids.shape[0] * BLK
+    picker = (slot_ids[:, None] == jnp.arange(lib_all.shape[0], dtype=jnp.int32)[None, :]).astype(
+        jnp.bfloat16
+    )
+    cached = jnp.dot(picker, lib_all, preferred_element_type=jnp.float32)
+    cached = cached.reshape(prefix_len, own).astype(jnp.bfloat16)
+    values = jnp.concatenate([cached, rows[prefix_len:, 2]], axis=0)
+    stacked = jnp.concatenate([rows[:, :2], values[:, None]], axis=1).astype(jnp.float32)
+
+    taps = lax.dynamic_slice_in_dim(short_taps, seq_index * own, own, axis=2)
+    gain = lax.dynamic_slice_in_dim(skip_gain, seq_index * own, own, axis=0)
+    shortened = jnp.zeros((tokens, 3, own), jnp.float32)
+    for offset in range(TAPS):
+        shifted = jnp.pad(stacked[: tokens - offset], ((offset, 0), (0, 0), (0, 0)))
+        shortened = shortened + taps[offset][None] * shifted
+    gating = shortened[:, 0]
+    signal = shortened[:, 1] * shortened[:, 2]
+
+    cos_t, sin_t = dft_tables(tokens)
+    table = jnp.concatenate([cos_t, sin_t], axis=0).astype(jnp.bfloat16)
+    operands = jnp.concatenate([signal.astype(jnp.bfloat16), rows[:, 3]], axis=1)
+    spec = jnp.dot(table, operands, preferred_element_type=jnp.float32)
+    bins = tokens + 1
+    sig_c, tap_c = spec[:bins, :own], spec[:bins, own:]
+    sig_s, tap_s = spec[bins:, :own], spec[bins:, own:]
+    weight = jnp.where(
+        (jnp.arange(bins) == 0) | (jnp.arange(bins) == tokens), 1.0, 2.0
+    ).astype(jnp.float32)[:, None] / (2 * tokens)
+    real = (sig_c * tap_c - sig_s * tap_s) * weight
+    turned = (sig_c * tap_s + sig_s * tap_c) * weight
+    back = jnp.concatenate([real, turned], axis=0).astype(jnp.bfloat16)
+    convolved = lax.dot_general(
+        table, back, (((0,), (0,)), ((), ())), preferred_element_type=jnp.float32
+    )
+    output = (gating * (convolved + gain[None, :] * signal)).astype(jnp.bfloat16)
+    return lax.all_to_all(output, "seq", split_axis=0, concat_axis=1, tiled=True)
+
+
+def body(fresh, library, *rest):
+    devices = lax.axis_size("seq")
+    tokens = fresh.shape[0] * devices
+    fits = tokens <= 4096 and fresh.shape[2] % devices == 0 and (library.shape[0] * BLK) % 4 == 0
+    if fits:
+        return local_body(fresh, library, *rest)
+    return ring_body(fresh, library, *rest)
+
+
 def solution(mesh):
     return jax.shard_map(
         body,

time: 218 us -> 87.2 us (0.40)
  blocking collectives: 105 us -> 12.5 us
  matrix products: 24.5 us -> 3.8 us
  starting transfers between devices: 21.6 us -> 7.41 us
  local copies, waits for them, and re-layouts: 23.8 us -> 12 us
  other arithmetic: 4.82 us -> 9.91 us
  waiting for transfers between devices: 37.5 us -> 40.9 us
    all_to_all x2 -> x1, blocking collectives: 67.5 us -> 12.5 us  [local_body(): lax.all_to_all(output, 'seq', split_axis=0, concat_axis=1, tiled=True)]
    all_gather x1 -> x0, blocking collectives: 37.2 us -> none  [body(): shards = lax.all_gather(library, 'seq', axis=0, tiled=True)]
    dot_general x19 -> x3, matrix products: 24.5 us -> 3.8 us  [the longest x1 2.2 us: local_body(): spec = jnp.dot(table, operands, preferred_element_type=jnp.float32)]
    all_to_all x4 -> x1, starting transfers between devices: 20.4 us -> 7.41 us  [local_body(): lax.all_to_all(packed, 'seq', split_axis=2, concat_axis=0, tiled=True)]
    another operation x3 -> x0, local copies, waits for them, and re-layouts: 7.3 us -> none  [the longest x1 4.15 us: body(): jnp.stack([back_real * back_cos - back_imag * back_sin, back_imag * back_...]
    all_to_all x4 -> x1, waiting for transfers between devices: 36.1 us -> 40.9 us  [local_body(): lax.all_to_all(packed, 'seq', split_axis=2, concat_axis=0, tiled=True)]
    slice x10 -> x4, local copies, waits for them, and re-layouts: 4.23 us -> 0.52 us  [the longest x2 0.48 us: local_body(): rows = moved[:, :row_count].reshape(tokens, 4, own)]
    squeeze x2, local copies, waits for them, and re-layouts: 3.63 us -> 0.03 us  [the longest x1 0.02 us: local_body(): rows[:, 3]]
  transfers between devices with their start and end apart: 5 -> 1, of which waited for: 4 -> 1; matrix products, arithmetic and copies ran while one was open for 7% -> 8% of each run, Pallas kernels for 0% -> 0%
where the time goes in v1:
time: 87.2 us; the launch traced here: 86.8 us
  waiting for transfers between devices  40.9 us (47%)
  blocking collectives  12.5 us (14%)
  local copies, waits for them, and re-layouts  12 us (14%)
  other arithmetic  9.91 us (11%)
  starting transfers between devices  7.41 us (8%)
  matrix products  3.8 us (4%)
    all_to_all x1, waiting for transfers between devices, local_body(): lax.all_to_all(packed, 'seq', split_axis=2, concat_axis=0, tiled=True)  40.9 us
    all_to_all x1, blocking collectives, local_body(): lax.all_to_all(output, 'seq', split_axis=0, concat_axis=1, tiled=True)  12.5 us
    all_to_all x1, starting transfers between devices, local_body(): lax.all_to_all(packed, 'seq', split_axis=2, concat_axis=0, tiled=True)  7.41 us
    another operation x2, other arithmetic  3.99 us
    all_to_all x1, local copies, waits for them, and re-layouts, local_body(): lax.all_to_all(packed, 'seq', split_axis=2, concat_axis=0, tiled=True)  3.92 us
    concatenate x1, other arithmetic, local_body(): jnp.concatenate([packed, library.reshape(lib_rows, 4, channels)], axis=0)  2.86 us
    unnamed x12, local copies, waits for them, and re-layouts  2.58 us
    dot_general x1, matrix products, local_body(): spec = jnp.dot(table, operands, preferred_element_type=jnp.float32)  2.2 us
  transfers between devices with their start and end apart: 1, of which 1 were waited for; matrix products, arithmetic and copies ran while one was open for 8% of the time, Pallas kernels for 0%

profile of v1, /device:TPU:0, one launch (start us, length us, event | category | flops | bytes accessed | tf_op | source)
XLA Modules:
  0.0 86.8 jit_solution(6593084510004803457)
XLA Ops:
  0.0 0.8 reshape.169
  0.8 1.1 %convert_bitcast_fusion = bf16[128,1,1024]{2,0,1:T(8,128)(2,1)S(1)} fusion(f32[128,1024]{1,0:T(8,128)} %param.12), kind=kLoop, calls=%fused_computation.27 | loop fusion | flops 131072 | bytes 786432 | tf_op jit(solution)/shard_map/broadcast_in_dim | solution.py:154
  1.9 0.4 copy.37
  2.3 0.7 copy.38
  3.1 0.7 copy.36
  3.8 2.9 %pad_maximum_fusion.3 = bf16[130,4,1024]{0,1,2:T(4,128)(2,1)} fusion(bf16[2,4,1024]{0,1,2:T(4,128)(2,1)S(1)} %copy.38, bf16[128,1,1024]{0,1,2:T(2,128)(2,1)S(1)} %copy.37, bf16[128,3,1024]{0,1,2:T(4,128)(2,1)S(1)} %copy.36), kind=kLoop, calls=%fused_computation.6 | loop fusion | flops 3194880 | bytes 2129920 | tf_op jit(solution)/shard_map/concatenate | solution.py:155
  6.7 7.4 %all-to-all-start = ((bf16[130,4,1024]{0,1,2:T(4,128)(2,1)}), bf16[130,4,1024]{0,1,2:T(4,128)(2,1)S(1)}, u32[]{:S(2)}, u32[]{:S(2)}) async-start(bf16[130,4,1024]{0,1,2:T(4,128)(2,1)} %pad_maximum_fusion.3), calls=%async_computation | async-start | bytes 4194304 | tf_op jit(solution)/shard_map/all_to_all | solution.py:156
  14.3 0.8 dynamic_slice.7
  15.0 0.7 gather_fusion
  15.7 0.7 dynamic-slice_bitcast_fusion.2
  16.5 0.6 fusion.25
  17.1 0.7 fusion.28
  17.7 3.7 %subtract_convert_fusion = (bf16[1025,32,32]{0,2,1:T(8,128)(2,1)}, bf16[1025,32,32]{0,2,1:T(8,128)(2,1)}) fusion(f32[1025,32]{0,1:T(8,128)S(1)} %get-tuple-element.14, f32[1025,32]{0,1:T(8,128)S(1)} %get-tuple-element.13, f32[1025,32]{0,1:T(8,128)S(1)} %get-tuple-element.15, f32[1025,32]{0,1:T(8,128)S(1)} %get-tuple-element.12), kind=kLoop, calls=%fused_computation.2 | loop fusion | flops 8396800 | bytes 4723200 | tf_op jit(solution)/shard_map/convert.5
  21.4 40.9 %all-to-all-done = bf16[130,4,1024]{0,1,2:T(4,128)(2,1)S(1)} async-done(((bf16[130,4,1024]{0,1,2:T(4,128)(2,1)}), bf16[130,4,1024]{0,1,2:T(4,128)(2,1)S(1)}, u32[]{:S(2)}, u32[]{:S(2)}) %all-to-all-start) | async-done | bytes 1064992 | tf_op jit(solution)/shard_map/all_to_all | solution.py:156
  62.3 3.9 %copy.43 = bf16[130,4,8,128]{3,2,1,0:T(8,128)(2,1)S(1)} copy(bf16[130,4,8,128]{0,1,3,2:T(4,128)(2,1)S(1)} %bitcast.44) | data formatting | bytes 2129920 | tf_op jit(solution)/shard_map/all_to_all | solution.py:156
  66.3 0.4 copy.40
  67.2 0.5 multiply_add_fusion
  67.9 1.0 %copy-done.1 = bf16[1025,32,32]{0,2,1:T(8,128)(2,1)S(1)} copy-done((bf16[1025,32,32]{0,2,1:T(8,128)(2,1)S(1)}, bf16[1025,32,32]{0,2,1:T(8,128)(2,1)}, u32[]{:S(2)}) %copy-start.1) | copy-done | bytes 2099224
  68.9 0.7 copy-done.2
  69.6 2.2 %fusion.1 = f32[2050,256]{1,0:T(8,128)S(1)} fusion(bf16[1025,1024]{0,1:T(8,128)(2,1)S(1)} %bitcast.52, bf16[1025,1024]{0,1:T(8,128)(2,1)S(1)} %bitcast.50, bf16[1024,128]{1,0:T(8,128)(2,1)S(1)} %slice_bitcast_fusion.1, bf16[1024,128]{1,0:T(8,128)(2,1)S(1)} %fusion.12), kind=kOutput, calls=%fused_computation.5 | convolution fusion | flops 1084235776 | bytes 6821888 | tf_op jit(solution)/shard_map/dot_general | solution.py:183
  71.8 0.3 multiply_convert_fusion.1
  72.1 1.4 %fusion.4 = bf16[1024,128]{1,0:T(8,128)(2,1)S(1)} fusion(bf16[1025,1024]{0,1:T(8,128)(2,1)S(1)} %bitcast.53, bf16[1025,1024]{0,1:T(8,128)(2,1)S(1)} %bitcast.51, bf16[1025,128]{1,0:T(8,128)(2,1)S(1)} %get-tuple-element.6, bf16[1025,128]{1,0:T(8,128)(2,1)S(1)} %get-tuple-element.5, f32[1024,3,128]{2,0,1:T(8,128)S(1)} %multiply_add_fusion, ...), kind=kOutput, calls=%fused_computation.10 | convolution fusion | flops 547496960 | bytes 6558720 | tf_op jit(solution)/shard_map/dot_general | solution.py:193
  73.5 12.5 %all_to_all.34 = bf16[8,128,128]{2,1,0:T(8,128)(2,1)S(1)} all-to-all(bf16[8,128,128]{2,1,0:T(8,128)(2,1)S(1)} %bitcast.54), channel_id=1, replica_groups=mesh['group'=2,'seq'=8,'chan'=2] {'seq'}, dimensions={0} | all-to-all | bytes 524288 | tf_op jit(solution)/shard_map/all_to_all | solution.py:197
  86.0 0.7 copy_bitcast_fusion
  (24 shorter events, 0.8 us)
Async XLA Ops:
  0.0 15.0 %copy-start = (s32[8]{0:T(128)S(1)}, s32[8]{0:T(128)}, u32[]{:S(2)}) copy-start(s32[8]{0:T(128)} %param.9) | copy-start | bytes 100
  0.0 3.1 %copy-start.3 = (bf16[128,3,1024]{2,0,1:T(8,128)(2,1)S(1)}, bf16[128,3,1024]{2,0,1:T(8,128)(2,1)}, u32[]{:S(2)}) copy-start(bf16[128,3,1024]{2,0,1:T(8,128)(2,1)} %param.7) | copy-start | bytes 2359300
  6.7 7.4 %copy-start.4 = (s32[8,4]{0,1:T(4,128)S(1)}, s32[8,4]{0,1:T(4,128)}, u32[]{:S(2)}) copy-start(s32[8,4]{0,1:T(4,128)} %param.10) | copy-start | bytes 388
  6.7 55.7 %all-to-all-start = ((bf16[130,4,1024]{0,1,2:T(4,128)(2,1)}), bf16[130,4,1024]{0,1,2:T(4,128)(2,1)S(1)}, u32[]{:S(2)}, u32[]{:S(2)}) async-start(bf16[130,4,1024]{0,1,2:T(4,128)(2,1)} %pad_maximum_fusion.3), calls=%async_computation | async-start | bytes 4194304 | tf_op jit(solution)/shard_map/all_to_all | solution.py:156
  67.2 1.7 %copy-start.1 = (bf16[1025,32,32]{0,2,1:T(8,128)(2,1)S(1)}, bf16[1025,32,32]{0,2,1:T(8,128)(2,1)}, u32[]{:S(2)}) copy-start(bf16[1025,32,32]{0,2,1:T(8,128)(2,1)} %get-tuple-element.7) | copy-start | bytes 6297604
  67.2 2.4 %copy-start.2 = (bf16[1025,32,32]{0,2,1:T(8,128)(2,1)S(1)}, bf16[1025,32,32]{0,2,1:T(8,128)(2,1)}, u32[]{:S(2)}) copy-start(bf16[1025,32,32]{0,2,1:T(8,128)(2,1)} %get-tuple-element.8) | copy-start | bytes 6297604

commit v2 on v1

--- a/solution.py
+++ b/solution.py
@@ -153,8 +153,8 @@
     lib_rows = lib_here * BLK // 4
     packed = jnp.concatenate([fresh, long_filter.astype(jnp.bfloat16)[:, None, :]], axis=1)
     packed = jnp.concatenate([packed, library.reshape(lib_rows, 4, channels)], axis=0)
-    moved = lax.all_to_all(packed, "seq", split_axis=2, concat_axis=0, tiled=True)
-    moved = moved.reshape(devices, row_count + lib_rows, 4, own)
+    packed = packed.reshape(row_count + lib_rows, 4, devices, own).transpose(2, 0, 1, 3)
+    moved = lax.all_to_all(packed, "seq", split_axis=0, concat_axis=0, tiled=True)
     rows = moved[:, :row_count].reshape(tokens, 4, own)
     lib_all = moved[:, row_count:].reshape(devices * lib_here, BLK * own)
 
@@ -194,7 +194,10 @@
         table, back, (((0,), (0,)), ((), ())), preferred_element_type=jnp.float32
     )
     output = (gating * (convolved + gain[None, :] * signal)).astype(jnp.bfloat16)
-    return lax.all_to_all(output, "seq", split_axis=0, concat_axis=1, tiled=True)
+    output = lax.all_to_all(
+        output.reshape(devices, row_count, own), "seq", split_axis=0, concat_axis=0, tiled=True
+    )
+    return output.transpose(1, 0, 2).reshape(row_count, channels)
 
 
 def body(fresh, library, *rest):

time: 87.2 us -> 63.3 us (0.73)
  waiting for transfers between devices: 40.9 us -> 18.8 us
  other arithmetic: 9.91 us -> 8.75 us
    all_to_all x1, waiting for transfers between devices: 40.9 us -> 18.8 us  [local_body(): lax.all_to_all(packed, 'seq', split_axis=0, concat_axis=0, tiled=True)]
    all_to_all x2 -> x0, local copies, waits for them, and re-layouts: 4.66 us -> none  [the longest x1 3.92 us: local_body(): lax.all_to_all(packed, 'seq', split_axis=2, concat_axis=0, tiled=True)]
    concatenate x1 -> x0, other arithmetic: 2.86 us -> none  [local_body(): jnp.concatenate([packed, library.reshape(lib_rows, 4, channels)], axis=0)]
    unnamed x12, local copies, waits for them, and re-layouts: 2.58 us -> 4.87 us
    transpose x0 -> x1, local copies, waits for them, and re-layouts: none -> 2.29 us  [local_body(): packed.reshape(row_count + lib_rows, 4, devices, own).transpose(2, 0, 1, 3)]
    transpose x0 -> x1, other arithmetic: none -> 1.7 us  [local_body(): packed.reshape(row_count + lib_rows, 4, devices, own).transpose(2, 0, 1, 3)]
    broadcast_in_dim x1 -> x0, other arithmetic: 1.07 us -> none  [local_body(): long_filter.astype(jnp.bfloat16)[:, None, :]]
    convert_element_type x0 -> x1, other arithmetic: none -> 1.07 us  [local_body(): long_filter.astype(jnp.bfloat16)[:, None, :]]
  transfers between devices with their start and end apart: 1 -> 1, of which waited for: 1 -> 1; matrix products, arithmetic and copies ran while one was open for 8% -> 12% of each run, Pallas kernels for 0% -> 0%
where the time goes in v2:
time: 63.3 us; the launch traced here: 62.9 us
  waiting for transfers between devices  18.8 us (30%)
  blocking collectives  12.5 us (20%)
  local copies, waits for them, and re-layouts  11.6 us (18%)
  other arithmetic  8.75 us (14%)
  starting transfers between devices  7.28 us (12%)
  matrix products  3.8 us (6%)
    all_to_all x1, waiting for transfers between devices, local_body(): lax.all_to_all(packed, 'seq', split_axis=0, concat_axis=0, tiled=True)  18.8 us
    all_to_all x1, blocking collectives, local_body(): lax.all_to_all(output.reshape(devices, row_count, own), 'seq', split_axis...  12.5 us
    all_to_all x1, starting transfers between devices, local_body(): lax.all_to_all(packed, 'seq', split_axis=0, concat_axis=0, tiled=True)  7.28 us
    unnamed x12, local copies, waits for them, and re-layouts  4.87 us
    another operation x2, other arithmetic  3.99 us
    transpose x1, local copies, waits for them, and re-layouts, local_body(): packed.reshape(row_count + lib_rows, 4, devices, own).transpose(2, 0, 1, 3)  2.29 us
    dot_general x1, matrix products, local_body(): spec = jnp.dot(table, operands, preferred_element_type=jnp.float32)  2.2 us
    transpose x1, other arithmetic, local_body(): packed.reshape(row_count + lib_rows, 4, devices, own).transpose(2, 0, 1, 3)  1.7 us
  transfers between devices with their start and end apart: 1, of which 1 were waited for; matrix products, arithmetic and copies ran while one was open for 12% of the time, Pallas kernels for 0%

profile of v2, /device:TPU:0, one launch (start us, length us, event | category | flops | bytes accessed | tf_op | source)
XLA Modules:
  0.0 62.9 jit_solution(6470833181533852721)
XLA Ops:
  0.0 0.7 %copy.40 = bf16[1,8,8,128]{3,2,1,0:T(8,128)(2,1)S(1)} copy(bf16[1,8,8,128]{3,1,2,0:T(8,128)(2,1)} %bitcast.60) | data formatting | bytes 32768
  0.7 1.1 %convert_element_type.49 = bf16[128,1024]{1,0:T(8,128)(2,1)S(1)} convert(f32[128,1024]{1,0:T(8,128)} %param.12) | non-fusion elementwise | flops 131072 | bytes 786432 | tf_op jit(solution)/shard_map/convert_element_type | solution.py:154
  2.0 2.3 %copy.30 = bf16[128,3,1024]{0,2,1:T(8,128)(2,1)} copy(bf16[128,3,1024]{2,0,1:T(8,128)(2,1)} %param.7) | data formatting | bytes 1572864 | tf_op args[0]
  4.3 0.5 copy.32
  4.8 1.7 %maximum_bitcast_fusion = bf16[8,130,4,128]{1,3,0,2:T(8,128)(2,1)S(1)} fusion(bf16[2,4,8,128]{0,3,2,1:T(8,128)(2,1)S(1)} %copy.32, bf16[128,1,8,128]{0,3,2,1:T(8,128)(2,1)S(1)} %bitcast.56, bf16[128,3,8,128]{0,3,2,1:T(8,128)(2,1)} %bitcast.51), kind=kLoop, calls=%fused_computation.6 | loop fusion | flops 3194880 | bytes 2129920 | tf_op jit(solution)/shard_map/transpose | solution.py:156
  6.5 2.3 %copy.33 = bf16[8,130,4,128]{3,2,1,0:T(4,128)(2,1)} copy(bf16[8,130,4,128]{1,3,0,2:T(8,128)(2,1)S(1)} %maximum_bitcast_fusion) | data formatting | bytes 2129920 | tf_op jit(solution)/shard_map/transpose | solution.py:156
  8.8 7.3 %all-to-all-start = ((bf16[8,130,4,128]{3,2,1,0:T(4,128)(2,1)}), bf16[8,130,4,128]{3,2,1,0:T(4,128)(2,1)S(1)}, u32[]{:S(2)}, u32[]{:S(2)}) async-start(bf16[8,130,4,128]{3,2,1,0:T(4,128)(2,1)} %copy.33), calls=%async_computation | async-start | bytes 2129920 | tf_op jit(solution)/shard_map/all_to_all | solution.py:157
  16.3 0.8 %dynamic_slice.7 = f32[128]{0:T(128)S(1)} dynamic-slice(f32[1024]{0:T(1024)} %param.13, s32[]{:T(128)S(6)} %select_n.53), dynamic_slice_sizes={128} | dynamic-slice | bytes 1028 | tf_op jit(solution)/shard_map/dynamic_slice | solution.py:172
  17.1 0.7 %gather_fusion = s32[32]{0:T(128)S(1)} fusion(s32[8]{0:T(128)S(1)} %copy-done, s32[1024]{0:T(1024)S(1)} %pad_clamp_fusion), kind=kCustom, calls=%fused_computation | custom fusion | bytes 384 | tf_op jit(solution)/shard_map/gather | solution.py:161
  17.8 0.7 %dynamic-slice_bitcast_fusion.2 = (f32[3,128]{1,0:T(4,128)S(1)}, f32[3,128]{1,0:T(4,128)S(1)}, f32[3,128]{1,0:T(4,128)S(1)}) fusion(f32[3,3,1024]{2,1,0:T(4,128)} %param.11, s32[]{:T(128)S(6)} %select_n.53, s32[]{:T(128)S(6)} %add.79, s32[]{:T(128)S(6)} %add.80), kind=kLoop, calls=%fused_computation.61 | loop fusion | bytes 9228 | tf_op jit(solution)/shard_map/mul | solution.py:176
  18.5 0.6 fusion.25
  19.1 0.7 %fusion.28 = (f32[1025,32]{0,1:T(8,128)S(1)}, f32[1025,32]{0,1:T(8,128)S(1)}) fusion(s32[32]{0:T(128)S(1)} %iota_multiply_fusion), kind=kLoop, calls=%fused_computation.50 | loop fusion | flops 459200 | bytes 262528 | tf_op jit(solution)/shard_map/cos | solution.py:139
  19.7 3.7 %subtract_convert_fusion = (bf16[1025,32,32]{0,2,1:T(8,128)(2,1)}, bf16[1025,32,32]{0,2,1:T(8,128)(2,1)}) fusion(f32[1025,32]{0,1:T(8,128)S(1)} %get-tuple-element.14, f32[1025,32]{0,1:T(8,128)S(1)} %get-tuple-element.13, f32[1025,32]{0,1:T(8,128)S(1)} %get-tuple-element.15, f32[1025,32]{0,1:T(8,128)S(1)} %get-tuple-element.12), kind=kLoop, calls=%fused_computation.2 | loop fusion | flops 8396800 | bytes 4723200 | tf_op jit(solution)/shard_map/convert.5
  23.4 18.8 %all-to-all-done = bf16[8,130,4,128]{3,2,1,0:T(4,128)(2,1)S(1)} async-done(((bf16[8,130,4,128]{3,2,1,0:T(4,128)(2,1)}), bf16[8,130,4,128]{3,2,1,0:T(4,128)(2,1)S(1)}, u32[]{:S(2)}, u32[]{:S(2)}) %all-to-all-start) | async-done | bytes 1064992 | tf_op jit(solution)/shard_map/all_to_all | solution.py:157
  42.2 0.4 slice.70
  42.6 0.2 copy.34
  43.4 0.5 multiply_add_fusion
  44.0 1.0 %copy-done.1 = bf16[1025,32,32]{0,2,1:T(8,128)(2,1)S(1)} copy-done((bf16[1025,32,32]{0,2,1:T(8,128)(2,1)S(1)}, bf16[1025,32,32]{0,2,1:T(8,128)(2,1)}, u32[]{:S(2)}) %copy-start.1) | copy-done | bytes 2099224
  45.0 0.7 %copy-done.2 = bf16[1025,32,32]{0,2,1:T(8,128)(2,1)S(1)} copy-done((bf16[1025,32,32]{0,2,1:T(8,128)(2,1)S(1)}, bf16[1025,32,32]{0,2,1:T(8,128)(2,1)}, u32[]{:S(2)}) %copy-start.2) | copy-done | bytes 2099224
  45.7 2.2 %fusion.1 = f32[2050,256]{1,0:T(8,128)S(1)} fusion(bf16[1025,1024]{0,1:T(8,128)(2,1)S(1)} %bitcast.54, bf16[1025,1024]{0,1:T(8,128)(2,1)S(1)} %bitcast.52, bf16[1024,128]{1,0:T(8,128)(2,1)S(1)} %slice_bitcast_fusion.1, bf16[1024,128]{1,0:T(8,128)(2,1)S(1)} %fusion.12), kind=kOutput, calls=%fused_computation.5 | convolution fusion | flops 1084235776 | bytes 6821888 | tf_op jit(solution)/shard_map/dot_general | solution.py:183
  47.9 0.3 multiply_convert_fusion.1
  48.2 1.4 %fusion.4 = bf16[1024,128]{1,0:T(8,128)(2,1)S(1)} fusion(bf16[1025,1024]{0,1:T(8,128)(2,1)S(1)} %bitcast.55, bf16[1025,1024]{0,1:T(8,128)(2,1)S(1)} %bitcast.53, bf16[1025,128]{1,0:T(8,128)(2,1)S(1)} %get-tuple-element.6, bf16[1025,128]{1,0:T(8,128)(2,1)S(1)} %get-tuple-element.5, f32[1024,3,128]{2,0,1:T(8,128)S(1)} %multiply_add_fusion, ...), kind=kOutput, calls=%fused_computation.10 | convolution fusion | flops 547496960 | bytes 6558720 | tf_op jit(solution)/shard_map/dot_general | solution.py:193
  49.6 12.5 %all_to_all.10 = bf16[8,128,128]{2,1,0:T(8,128)(2,1)S(1)} all-to-all(bf16[8,128,128]{2,1,0:T(8,128)(2,1)S(1)} %bitcast.57), channel_id=1, replica_groups=mesh['group'=2,'seq'=8,'chan'=2] {'seq'}, dimensions={0} | all-to-all | bytes 524288 | tf_op jit(solution)/shard_map/all_to_all | solution.py:197
  62.1 0.7 %copy_bitcast_fusion = bf16[128,1024]{1,0:T(8,128)(2,1)} fusion(bf16[8,128,128]{2,1,0:T(8,128)(2,1)S(1)} %all_to_all.10), kind=kLoop, calls=%fused_computation.24 | loop fusion | bytes 524288 | tf_op jit(solution)/shard_map/reshape | solution.py:200
  (23 shorter events, 0.9 us)
Async XLA Ops:
  0.0 17.0 %copy-start = (s32[8]{0:T(128)S(1)}, s32[8]{0:T(128)}, u32[]{:S(2)}) copy-start(s32[8]{0:T(128)} %param.9) | copy-start | bytes 100
  6.5 9.6 %copy-start.3 = (s32[8,4]{0,1:T(4,128)S(1)}, s32[8,4]{0,1:T(4,128)}, u32[]{:S(2)}) copy-start(s32[8,4]{0,1:T(4,128)} %param.10) | copy-start | bytes 388
  8.8 33.4 %all-to-all-start = ((bf16[8,130,4,128]{3,2,1,0:T(4,128)(2,1)}), bf16[8,130,4,128]{3,2,1,0:T(4,128)(2,1)S(1)}, u32[]{:S(2)}, u32[]{:S(2)}) async-start(bf16[8,130,4,128]{3,2,1,0:T(4,128)(2,1)} %copy.33), calls=%async_computation | async-start | bytes 2129920 | tf_op jit(solution)/shard_map/all_to_all | solution.py:157
  43.3 1.7 %copy-start.1 = (bf16[1025,32,32]{0,2,1:T(8,128)(2,1)S(1)}, bf16[1025,32,32]{0,2,1:T(8,128)(2,1)}, u32[]{:S(2)}) copy-start(bf16[1025,32,32]{0,2,1:T(8,128)(2,1)} %get-tuple-element.7) | copy-start | bytes 6297604
  43.3 2.4 %copy-start.2 = (bf16[1025,32,32]{0,2,1:T(8,128)(2,1)S(1)}, bf16[1025,32,32]{0,2,1:T(8,128)(2,1)}, u32[]{:S(2)}) copy-start(bf16[1025,32,32]{0,2,1:T(8,128)(2,1)} %get-tuple-element.8) | copy-start | bytes 6297604

commit v3 on v2

--- a/solution.py
+++ b/solution.py
@@ -127,6 +127,21 @@
     return output.astype(jnp.bfloat16)
 
 
+def exchange(chunk_of, devices):
+    seq_index = lax.axis_index("seq")
+    arrived = []
+    for shift in range(devices):
+        block = chunk_of(lax.rem(seq_index + shift, devices))
+        if shift:
+            block = lax.ppermute(
+                block, "seq", [(i, (i + shift) % devices) for i in range(devices)]
+            )
+        arrived.append(block)
+    turned = jnp.stack(arrived[::-1] * 2)
+    start = lax.rem(devices - 1 - seq_index + devices, devices)
+    return lax.dynamic_slice_in_dim(turned, start, devices, axis=0)
+
+
 def dft_tables(tokens):
     period = 2 * tokens
     width = 1
@@ -153,8 +168,9 @@
     lib_rows = lib_here * BLK // 4
     packed = jnp.concatenate([fresh, long_filter.astype(jnp.bfloat16)[:, None, :]], axis=1)
     packed = jnp.concatenate([packed, library.reshape(lib_rows, 4, channels)], axis=0)
-    packed = packed.reshape(row_count + lib_rows, 4, devices, own).transpose(2, 0, 1, 3)
-    moved = lax.all_to_all(packed, "seq", split_axis=0, concat_axis=0, tiled=True)
+    moved = exchange(
+        lambda d: lax.dynamic_slice_in_dim(packed, d * own, own, axis=2), devices
+    )
     rows = moved[:, :row_count].reshape(tokens, 4, own)
     lib_all = moved[:, row_count:].reshape(devices * lib_here, BLK * own)
 
@@ -194,8 +210,8 @@
         table, back, (((0,), (0,)), ((), ())), preferred_element_type=jnp.float32
     )
     output = (gating * (convolved + gain[None, :] * signal)).astype(jnp.bfloat16)
-    output = lax.all_to_all(
-        output.reshape(devices, row_count, own), "seq", split_axis=0, concat_axis=0, tiled=True
+    output = exchange(
+        lambda d: lax.dynamic_slice_in_dim(output, d * row_count, row_count, axis=0), devices
     )
     return output.transpose(1, 0, 2).reshape(row_count, channels)
 

time: 63.3 us -> 70.2 us (1.11)
  starting transfers between devices: 7.28 us -> 30.6 us
  blocking collectives: 12.5 us -> 0 us
  waiting for transfers between devices: 18.8 us -> 15.9 us
  local copies, waits for them, and re-layouts: 11.6 us -> 9.83 us
    ppermute x0 -> x14, starting transfers between devices: none -> 30.6 us  [exchange(): lax.ppermute(block, 'seq', [(i, (i + shift) % devices) for i in range(dev...]
    all_to_all x1 -> x0, waiting for transfers between devices: 18.8 us -> none  [local_body(): lax.all_to_all(packed, 'seq', split_axis=0, concat_axis=0, tiled=True)]
    ppermute x0 -> x14, waiting for transfers between devices: none -> 15.9 us  [exchange(): lax.ppermute(block, 'seq', [(i, (i + shift) % devices) for i in range(dev...]
    all_to_all x1 -> x0, blocking collectives: 12.5 us -> none  [local_body(): lax.all_to_all(output.reshape(devices, row_count, own), 'seq', split_axis...]
    all_to_all x1 -> x0, starting transfers between devices: 7.28 us -> none  [local_body(): lax.all_to_all(packed, 'seq', split_axis=0, concat_axis=0, tiled=True)]
    transpose x1 -> x0, local copies, waits for them, and re-layouts: 2.29 us -> none  [local_body(): packed.reshape(row_count + lib_rows, 4, devices, own).transpose(2, 0, 1, 3)]
    unnamed x12 -> x41, local copies, waits for them, and re-layouts: 4.87 us -> 3.07 us
    transpose x1 -> x0, other arithmetic: 1.7 us -> none  [local_body(): packed.reshape(row_count + lib_rows, 4, devices, own).transpose(2, 0, 1, 3)]
  transfers between devices with their start and end apart: 1 -> 14, of which waited for: 1 -> 4; matrix products, arithmetic and copies ran while one was open for 12% -> 11% of each run, Pallas kernels for 0% -> 0%
where the time goes in v3:
time: 70.2 us; the launch traced here: 69.9 us
  starting transfers between devices  30.6 us (44%)
  waiting for transfers between devices  15.9 us (23%)
  local copies, waits for them, and re-layouts  9.83 us (14%)
  other arithmetic  9.03 us (13%)
  matrix products  4.07 us (6%)
    ppermute x14, starting transfers between devices, exchange(): lax.ppermute(block, 'seq', [(i, (i + shift) % devices) for i in range(dev...  30.6 us
    ppermute x14, waiting for transfers between devices, exchange(): lax.ppermute(block, 'seq', [(i, (i + shift) % devices) for i in range(dev...  15.9 us
    another operation x2, other arithmetic  3.99 us
    unnamed x41, local copies, waits for them, and re-layouts  3.07 us
    dot_general x1, matrix products, local_body(): spec = jnp.dot(table, operands, preferred_element_type=jnp.float32)  2.19 us
    dot_general x1, matrix products, local_body(): lax.dot_general(table, back, (((0,), (0,)), ((), ())), preferred_element_...  1.67 us
  transfers between devices with their start and end apart: 14, of which 4 were waited for; matrix products, arithmetic and copies ran while one was open for 11% of the time, Pallas kernels for 0%

profile of v3, /device:TPU:0, one launch (start us, length us, event | category | flops | bytes accessed | tf_op | source)
XLA Modules:
  0.0 69.9 jit_solution(3409314783963283844)
XLA Ops:
  0.8 1.1 %convert_bitcast_fusion = bf16[128,1,1024]{2,0,1:T(8,128)(2,1)S(1)} fusion(f32[128,1024]{1,0:T(8,128)} %param.12), kind=kLoop, calls=%fused_computation.26 | loop fusion | flops 131072 | bytes 786432 | tf_op jit(solution)/shard_map/broadcast_in_dim | solution.py:169
  1.9 1.3 %pad_maximum_fusion.9 = bf16[130,4,1024]{2,0,1:T(8,128)(2,1)S(1)} fusion(bf16[2,4,1024]{2,0,1:T(2,128)(2,1)S(1)} %copy.35, bf16[128,1,1024]{2,0,1:T(8,128)(2,1)S(1)} %convert_bitcast_fusion, bf16[128,3,1024]{2,0,1:T(8,128)(2,1)} %param.7), kind=kLoop, calls=%fused_computation.11 | loop fusion | flops 3194880 | bytes 2129920 | tf_op jit(solution)/shard_map/concatenate | solution.py:170
  3.5 3.0 %collective-permute-start.6 = (bf16[130,4,128]{2,0,1:T(8,128)(2,1)S(1)}, bf16[130,4,128]{2,0,1:T(8,128)(2,1)S(1)}, u32[]{:S(2)}, u32[]{:S(2)}) collective-permute-start(bf16[130,4,128]{2,0,1:T(8,128)(2,1)S(1)} %get-tuple-element.7), channel_id=1, source_target_pairs={{0,2},{2,4},{4,6},{6,8},{8,10},{10,12},{12,14},{14,0},{1,3},{3,5},... | collective-permute-start | bytes 399368 | tf_op jit(solution)/shard_map/ppermute | solution.py:136
  6.5 1.6 %collective-permute-start.5 = (bf16[130,4,128]{2,0,1:T(8,128)(2,1)S(1)}, bf16[130,4,128]{2,0,1:T(8,128)(2,1)S(1)}, u32[]{:S(2)}, u32[]{:S(2)}) collective-permute-start(bf16[130,4,128]{2,0,1:T(8,128)(2,1)S(1)} %get-tuple-element.8), channel_id=1, source_target_pairs={{0,4},{2,6},{4,8},{6,10},{8,12},{10,14},{12,0},{14,2},{1,5},{3,7},... | collective-permute-start | bytes 399368 | tf_op jit(solution)/shard_map/ppermute | solution.py:136
  8.1 2.6 %collective-permute-start.4 = (bf16[130,4,128]{2,0,1:T(8,128)(2,1)S(1)}, bf16[130,4,128]{2,0,1:T(8,128)(2,1)S(1)}, u32[]{:S(2)}, u32[]{:S(2)}) collective-permute-start(bf16[130,4,128]{2,0,1:T(8,128)(2,1)S(1)} %get-tuple-element.9), channel_id=1, source_target_pairs={{0,6},{2,8},{4,10},{6,12},{8,14},{10,0},{12,2},{14,4},{1,7},{3,9},... | collective-permute-start | bytes 399368 | tf_op jit(solution)/shard_map/ppermute | solution.py:136
  10.6 1.2 %collective-permute-start.3 = (bf16[130,4,128]{2,0,1:T(8,128)(2,1)S(1)}, bf16[130,4,128]{2,0,1:T(8,128)(2,1)S(1)}, u32[]{:S(2)}, u32[]{:S(2)}) collective-permute-start(bf16[130,4,128]{2,0,1:T(8,128)(2,1)S(1)} %get-tuple-element.10), channel_id=1, source_target_pairs={{0,8},{2,10},{4,12},{6,14},{8,0},{10,2},{12,4},{14,6},{1,9},{3,11}... | collective-permute-start | bytes 399368 | tf_op jit(solution)/shard_map/ppermute | solution.py:136
  11.9 2.3 %collective-permute-start = (bf16[130,4,128]{2,0,1:T(8,128)(2,1)S(1)}, bf16[130,4,128]{2,0,1:T(8,128)(2,1)S(1)}, u32[]{:S(2)}, u32[]{:S(2)}) collective-permute-start(bf16[130,4,128]{2,0,1:T(8,128)(2,1)S(1)} %get-tuple-element.13), channel_id=1, source_target_pairs={{0,14},{2,0},{4,2},{6,4},{8,6},{10,8},{12,10},{14,12},{1,15},{3,1}... | collective-permute-start | bytes 399368 | tf_op jit(solution)/shard_map/ppermute | solution.py:136
  16.3 3.7 %subtract_convert_fusion = (bf16[1025,32,32]{0,2,1:T(8,128)(2,1)}, bf16[1025,32,32]{0,2,1:T(8,128)(2,1)}) fusion(f32[1025,32]{0,1:T(8,128)S(1)} %get-tuple-element.28, f32[1025,32]{0,1:T(8,128)S(1)} %get-tuple-element.27, f32[1025,32]{0,1:T(8,128)S(1)} %get-tuple-element.29, f32[1025,32]{0,1:T(8,128)S(1)} %get-tuple-element.26), kind=kLoop, calls=%fused_computation.2 | loop fusion | flops 8396800 | bytes 4723200 | tf_op jit(solution)/shard_map/convert.5
  21.5 1.9 %collective-permute-start.1 = (bf16[130,4,128]{2,0,1:T(8,128)(2,1)S(1)}, bf16[130,4,128]{2,0,1:T(8,128)(2,1)S(1)}, u32[]{:S(2)}, u32[]{:S(2)}) collective-permute-start(bf16[130,4,128]{2,0,1:T(8,128)(2,1)S(1)} %get-tuple-element.12), channel_id=1, source_target_pairs={{0,12},{2,14},{4,0},{6,2},{8,4},{10,6},{12,8},{14,10},{1,13},{3,15... | collective-permute-start | bytes 399368 | tf_op jit(solution)/shard_map/ppermute | solution.py:136
  23.4 3.2 %collective-permute-done.1 = bf16[130,4,128]{2,0,1:T(8,128)(2,1)S(1)} collective-permute-done((bf16[130,4,128]{2,0,1:T(8,128)(2,1)S(1)}, bf16[130,4,128]{2,0,1:T(8,128)(2,1)S(1)}, u32[]{:S(2)}, u32[]{:S(2)}) %collective-permute-start.1) | collective-permute-done | bytes 133152 | tf_op jit(solution)/shard_map/ppermute | solution.py:136
  26.6 5.1 %collective-permute-start.2 = (bf16[130,4,128]{2,0,1:T(8,128)(2,1)S(1)}, bf16[130,4,128]{2,0,1:T(8,128)(2,1)S(1)}, u32[]{:S(2)}, u32[]{:S(2)}) collective-permute-start(bf16[130,4,128]{2,0,1:T(8,128)(2,1)S(1)} %get-tuple-element.11), channel_id=1, source_target_pairs={{0,10},{2,12},{4,14},{6,0},{8,2},{10,4},{12,6},{14,8},{1,11},{3,13... | collective-permute-start | bytes 399368 | tf_op jit(solution)/shard_map/ppermute | solution.py:136
  31.7 4.0 %collective-permute-done.2 = bf16[130,4,128]{2,0,1:T(8,128)(2,1)S(1)} collective-permute-done((bf16[130,4,128]{2,0,1:T(8,128)(2,1)S(1)}, bf16[130,4,128]{2,0,1:T(8,128)(2,1)S(1)}, u32[]{:S(2)}, u32[]{:S(2)}) %collective-permute-start.2) | collective-permute-done | bytes 133152 | tf_op jit(solution)/shard_map/ppermute | solution.py:136
  36.2 1.4 %copy-done.3 = bf16[16,130,4,128]{3,1,2,0:T(8,128)(2,1)} copy-done((bf16[16,130,4,128]{3,1,2,0:T(8,128)(2,1)}, bf16[16,130,4,128]{3,1,2,0:T(8,128)(2,1)S(1)}, u32[]{:S(2)}) %copy-start.3) | copy-done | bytes 2129944
  39.1 0.9 %constant_dynamic-slice_fusion.11 = bf16[8,2,4,128]{3,1,2,0:T(2,128)(2,1)S(1)} fusion(bf16[16,130,4,128]{3,1,2,0:T(8,128)(2,1)} %copy-done.3, s32[]{:T(128)S(6)} %select_n.98, s32[]{:T(128)S(6)} %add.165), kind=kLoop, calls=%fused_computation.100 | loop fusion | bytes 32776 | tf_op jit(solution)/shard_map/slice | solution.py:175
  40.5 1.2 %multiply_add_fusion = f32[1024,3,128]{0,2,1:T(8,128)S(1)} fusion(f32[1022,3,128]{0,2,1:T(8,128)S(1)} %bitcast.87, f32[1023,3,128]{0,2,1:T(8,128)S(1)} %bitcast.88, f32[3,128]{1,0:T(4,128)S(1)} %get-tuple-element.25, f32[3,128]{1,0:T(4,128)S(1)} %get-tuple-element.24, f32[3,128]{1,0:T(4,128)S(1)} %get-tuple-element.23, ...), kind=kLoop, calls=%fused_computation.6 | loop fusion | flops 2752512 | bytes 5505024 | tf_op jit(solution)/shard_map/add | solution.py:192
  42.8 2.2 %fusion.1 = f32[2050,256]{1,0:T(8,128)S(1)} fusion(bf16[1025,1024]{0,1:T(8,128)(2,1)S(1)} %bitcast.91, bf16[1025,1024]{0,1:T(8,128)(2,1)S(1)} %bitcast.89, bf16[1024,128]{0,1:T(8,128)(2,1)S(1)} %slice_bitcast_fusion.1, bf16[1024,128]{0,1:T(8,128)(2,1)S(1)} %fusion.12), kind=kOutput, calls=%fused_computation.5 | convolution fusion | flops 1084235776 | bytes 6821888 | tf_op jit(solution)/shard_map/dot_general | solution.py:199
  45.3 1.7 %fusion.4 = bf16[1024,128]{0,1:T(8,128)(2,1)S(1)} fusion(bf16[1025,1024]{0,1:T(8,128)(2,1)S(1)} %bitcast.92, bf16[1025,1024]{0,1:T(8,128)(2,1)S(1)} %bitcast.90, bf16[1025,128]{1,0:T(8,128)(2,1)S(1)} %get-tuple-element.6, bf16[1025,128]{1,0:T(8,128)(2,1)S(1)} %get-tuple-element.5, f32[1024,3,128]{0,2,1:T(8,128)S(1)} %multiply_add_fusion, ...), kind=kOutput, calls=%fused_computation.9 | convolution fusion | flops 547496960 | bytes 6558720 | tf_op jit(solution)/shard_map/dot_general | solution.py:209
  47.1 4.8 %collective-permute-start.7 = (bf16[128,128]{0,1:T(8,128)(2,1)S(1)}, bf16[128,128]{0,1:T(8,128)(2,1)S(1)}, u32[]{:S(2)}, u32[]{:S(2)}) collective-permute-start(bf16[128,128]{0,1:T(8,128)(2,1)S(1)} %get-tuple-element.22), channel_id=1, source_target_pairs={{0,14},{2,0},{4,2},{6,4},{8,6},{10,8},{12,10},{14,12},{1,15},{3,1}... | collective-permute-start | bytes 98312 | tf_op jit(solution)/shard_map/ppermute | solution.py:136
  51.9 1.4 %collective-permute-start.13 = (bf16[128,128]{0,1:T(8,128)(2,1)S(1)}, bf16[128,128]{0,1:T(8,128)(2,1)S(1)}, u32[]{:S(2)}, u32[]{:S(2)}) collective-permute-start(bf16[128,128]{0,1:T(8,128)(2,1)S(1)} %get-tuple-element.16), channel_id=1, source_target_pairs={{0,2},{2,4},{4,6},{6,8},{8,10},{10,12},{12,14},{14,0},{1,3},{3,5},... | collective-permute-start | bytes 98312 | tf_op jit(solution)/shard_map/ppermute | solution.py:136
  53.3 1.4 %collective-permute-start.12 = (bf16[128,128]{0,1:T(8,128)(2,1)S(1)}, bf16[128,128]{0,1:T(8,128)(2,1)S(1)}, u32[]{:S(2)}, u32[]{:S(2)}) collective-permute-start(bf16[128,128]{0,1:T(8,128)(2,1)S(1)} %get-tuple-element.17), channel_id=1, source_target_pairs={{0,4},{2,6},{4,8},{6,10},{8,12},{10,14},{12,0},{14,2},{1,5},{3,7},... | collective-permute-start | bytes 98312 | tf_op jit(solution)/shard_map/ppermute | solution.py:136
  54.7 5.3 %collective-permute-start.10 = (bf16[128,128]{0,1:T(8,128)(2,1)S(1)}, bf16[128,128]{0,1:T(8,128)(2,1)S(1)}, u32[]{:S(2)}, u32[]{:S(2)}) collective-permute-start(bf16[128,128]{0,1:T(8,128)(2,1)S(1)} %get-tuple-element.19), channel_id=1, source_target_pairs={{0,8},{2,10},{4,12},{6,14},{8,0},{10,2},{12,4},{14,6},{1,9},{3,11}... | collective-permute-start | bytes 98312 | tf_op jit(solution)/shard_map/ppermute | solution.py:136
  60.1 3.8 %collective-permute-done.8 = bf16[128,128]{0,1:T(8,128)(2,1)S(1)} collective-permute-done((bf16[128,128]{0,1:T(8,128)(2,1)S(1)}, bf16[128,128]{0,1:T(8,128)(2,1)S(1)}, u32[]{:S(2)}, u32[]{:S(2)}) %collective-permute-start.8) | collective-permute-done | bytes 32800 | tf_op jit(solution)/shard_map/ppermute | solution.py:136
  63.9 4.8 %collective-permute-done.9 = bf16[128,128]{0,1:T(8,128)(2,1)S(1)} collective-permute-done((bf16[128,128]{0,1:T(8,128)(2,1)S(1)}, bf16[128,128]{0,1:T(8,128)(2,1)S(1)}, u32[]{:S(2)}, u32[]{:S(2)}) %collective-permute-start.9) | collective-permute-done | bytes 32800 | tf_op jit(solution)/shard_map/ppermute | solution.py:136
  69.0 0.9 %copy.40 = bf16[128,1024]{1,0:T(8,128)(2,1)} copy(bf16[128,1024]{0,1:T(8,128)(2,1)S(1)} %bitcast.93) | data formatting | bytes 524288 | tf_op jit(solution)/shard_map/reshape | solution.py:216
  (84 shorter events, 8.8 us)
Async XLA Ops:
  0.0 20.8 %copy-start = (s32[8]{0:T(128)S(1)}, s32[8]{0:T(128)}, u32[]{:S(2)}) copy-start(s32[8]{0:T(128)} %param.9) | copy-start | bytes 100
  1.9 12.8 %copy-start.4 = (s32[8,4]{0,1:T(4,128)S(1)}, s32[8,4]{0,1:T(4,128)}, u32[]{:S(2)}) copy-start(s32[8,4]{0,1:T(4,128)} %param.10) | copy-start | bytes 388
  3.5 32.4 %collective-permute-start.6 = (bf16[130,4,128]{2,0,1:T(8,128)(2,1)S(1)}, bf16[130,4,128]{2,0,1:T(8,128)(2,1)S(1)}, u32[]{:S(2)}, u32[]{:S(2)}) collective-permute-start(bf16[130,4,128]{2,0,1:T(8,128)(2,1)S(1)} %get-tuple-element.7), channel_id=1, source_target_pairs={{0,2},{2,4},{4,6},{6,8},{8,10},{10,12},{12,14},{14,0},{1,3},{3,5},... | collective-permute-start | bytes 399368 | tf_op jit(solution)/shard_map/ppermute | solution.py:136
  6.5 29.3 %collective-permute-start.5 = (bf16[130,4,128]{2,0,1:T(8,128)(2,1)S(1)}, bf16[130,4,128]{2,0,1:T(8,128)(2,1)S(1)}, u32[]{:S(2)}, u32[]{:S(2)}) collective-permute-start(bf16[130,4,128]{2,0,1:T(8,128)(2,1)S(1)} %get-tuple-element.8), channel_id=1, source_target_pairs={{0,4},{2,6},{4,8},{6,10},{8,12},{10,14},{12,0},{14,2},{1,5},{3,7},... | collective-permute-start | bytes 399368 | tf_op jit(solution)/shard_map/ppermute | solution.py:136
  8.1 27.7 %collective-permute-start.4 = (bf16[130,4,128]{2,0,1:T(8,128)(2,1)S(1)}, bf16[130,4,128]{2,0,1:T(8,128)(2,1)S(1)}, u32[]{:S(2)}, u32[]{:S(2)}) collective-permute-start(bf16[130,4,128]{2,0,1:T(8,128)(2,1)S(1)} %get-tuple-element.9), channel_id=1, source_target_pairs={{0,6},{2,8},{4,10},{6,12},{8,14},{10,0},{12,2},{14,4},{1,7},{3,9},... | collective-permute-start | bytes 399368 | tf_op jit(solution)/shard_map/ppermute | solution.py:136
  10.6 25.1 %collective-permute-start.3 = (bf16[130,4,128]{2,0,1:T(8,128)(2,1)S(1)}, bf16[130,4,128]{2,0,1:T(8,128)(2,1)S(1)}, u32[]{:S(2)}, u32[]{:S(2)}) collective-permute-start(bf16[130,4,128]{2,0,1:T(8,128)(2,1)S(1)} %get-tuple-element.10), channel_id=1, source_target_pairs={{0,8},{2,10},{4,12},{6,14},{8,0},{10,2},{12,4},{14,6},{1,9},{3,11}... | collective-permute-start | bytes 399368 | tf_op jit(solution)/shard_map/ppermute | solution.py:136
  11.9 9.6 %collective-permute-start = (bf16[130,4,128]{2,0,1:T(8,128)(2,1)S(1)}, bf16[130,4,128]{2,0,1:T(8,128)(2,1)S(1)}, u32[]{:S(2)}, u32[]{:S(2)}) collective-permute-start(bf16[130,4,128]{2,0,1:T(8,128)(2,1)S(1)} %get-tuple-element.13), channel_id=1, source_target_pairs={{0,14},{2,0},{4,2},{6,4},{8,6},{10,8},{12,10},{14,12},{1,15},{3,1}... | collective-permute-start | bytes 399368 | tf_op jit(solution)/shard_map/ppermute | solution.py:136
  21.5 5.1 %collective-permute-start.1 = (bf16[130,4,128]{2,0,1:T(8,128)(2,1)S(1)}, bf16[130,4,128]{2,0,1:T(8,128)(2,1)S(1)}, u32[]{:S(2)}, u32[]{:S(2)}) collective-permute-start(bf16[130,4,128]{2,0,1:T(8,128)(2,1)S(1)} %get-tuple-element.12), channel_id=1, source_target_pairs={{0,12},{2,14},{4,0},{6,2},{8,4},{10,6},{12,8},{14,10},{1,13},{3,15... | collective-permute-start | bytes 399368 | tf_op jit(solution)/shard_map/ppermute | solution.py:136
  26.6 9.1 %collective-permute-start.2 = (bf16[130,4,128]{2,0,1:T(8,128)(2,1)S(1)}, bf16[130,4,128]{2,0,1:T(8,128)(2,1)S(1)}, u32[]{:S(2)}, u32[]{:S(2)}) collective-permute-start(bf16[130,4,128]{2,0,1:T(8,128)(2,1)S(1)} %get-tuple-element.11), channel_id=1, source_target_pairs={{0,10},{2,12},{4,14},{6,0},{8,2},{10,4},{12,6},{14,8},{1,11},{3,13... | collective-permute-start | bytes 399368 | tf_op jit(solution)/shard_map/ppermute | solution.py:136
  36.2 1.4 %copy-start.3 = (bf16[16,130,4,128]{3,1,2,0:T(8,128)(2,1)}, bf16[16,130,4,128]{3,1,2,0:T(8,128)(2,1)S(1)}, u32[]{:S(2)}) copy-start(bf16[16,130,4,128]{3,1,2,0:T(8,128)(2,1)S(1)} %bitcast_dynamic-update-slice_fusion.1) | copy-start | bytes 6389764
  40.5 1.7 %copy-start.1 = (bf16[1025,32,32]{0,2,1:T(8,128)(2,1)S(1)}, bf16[1025,32,32]{0,2,1:T(8,128)(2,1)}, u32[]{:S(2)}) copy-start(bf16[1025,32,32]{0,2,1:T(8,128)(2,1)} %get-tuple-element.14) | copy-start | bytes 6297604
  40.5 2.4 %copy-start.2 = (bf16[1025,32,32]{0,2,1:T(8,128)(2,1)S(1)}, bf16[1025,32,32]{0,2,1:T(8,128)(2,1)}, u32[]{:S(2)}) copy-start(bf16[1025,32,32]{0,2,1:T(8,128)(2,1)} %get-tuple-element.15) | copy-start | bytes 6297604
  47.1 12.9 %collective-permute-start.7 = (bf16[128,128]{0,1:T(8,128)(2,1)S(1)}, bf16[128,128]{0,1:T(8,128)(2,1)S(1)}, u32[]{:S(2)}, u32[]{:S(2)}) collective-permute-start(bf16[128,128]{0,1:T(8,128)(2,1)S(1)} %get-tuple-element.22), channel_id=1, source_target_pairs={{0,14},{2,0},{4,2},{6,4},{8,6},{10,8},{12,10},{14,12},{1,15},{3,1}... | collective-permute-start | bytes 98312 | tf_op jit(solution)/shard_map/ppermute | solution.py:136
  51.9 16.9 %collective-permute-start.13 = (bf16[128,128]{0,1:T(8,128)(2,1)S(1)}, bf16[128,128]{0,1:T(8,128)(2,1)S(1)}, u32[]{:S(2)}, u32[]{:S(2)}) collective-permute-start(bf16[128,128]{0,1:T(8,128)(2,1)S(1)} %get-tuple-element.16), channel_id=1, source_target_pairs={{0,2},{2,4},{4,6},{6,8},{8,10},{10,12},{12,14},{14,0},{1,3},{3,5},... | collective-permute-start | bytes 98312 | tf_op jit(solution)/shard_map/ppermute | solution.py:136
  53.3 15.5 %collective-permute-start.12 = (bf16[128,128]{0,1:T(8,128)(2,1)S(1)}, bf16[128,128]{0,1:T(8,128)(2,1)S(1)}, u32[]{:S(2)}, u32[]{:S(2)}) collective-permute-start(bf16[128,128]{0,1:T(8,128)(2,1)S(1)} %get-tuple-element.17), channel_id=1, source_target_pairs={{0,4},{2,6},{4,8},{6,10},{8,12},{10,14},{12,0},{14,2},{1,5},{3,7},... | collective-permute-start | bytes 98312 | tf_op jit(solution)/shard_map/ppermute | solution.py:136
  54.7 14.0 %collective-permute-start.11 = (bf16[128,128]{0,1:T(8,128)(2,1)S(1)}, bf16[128,128]{0,1:T(8,128)(2,1)S(1)}, u32[]{:S(2)}, u32[]{:S(2)}) collective-permute-start(bf16[128,128]{0,1:T(8,128)(2,1)S(1)} %get-tuple-element.18), channel_id=1, source_target_pairs={{0,6},{2,8},{4,10},{6,12},{8,14},{10,0},{12,2},{14,4},{1,7},{3,9},... | collective-permute-start | bytes 98312 | tf_op jit(solution)/shard_map/ppermute | solution.py:136
  54.7 14.0 %collective-permute-start.10 = (bf16[128,128]{0,1:T(8,128)(2,1)S(1)}, bf16[128,128]{0,1:T(8,128)(2,1)S(1)}, u32[]{:S(2)}, u32[]{:S(2)}) collective-permute-start(bf16[128,128]{0,1:T(8,128)(2,1)S(1)} %get-tuple-element.19), channel_id=1, source_target_pairs={{0,8},{2,10},{4,12},{6,14},{8,0},{10,2},{12,4},{14,6},{1,9},{3,11}... | collective-permute-start | bytes 98312 | tf_op jit(solution)/shard_map/ppermute | solution.py:136
  60.0 3.9 %collective-permute-start.8 = (bf16[128,128]{0,1:T(8,128)(2,1)S(1)}, bf16[128,128]{0,1:T(8,128)(2,1)S(1)}, u32[]{:S(2)}, u32[]{:S(2)}) collective-permute-start(bf16[128,128]{0,1:T(8,128)(2,1)S(1)} %get-tuple-element.21), channel_id=1, source_target_pairs={{0,12},{2,14},{4,0},{6,2},{8,4},{10,6},{12,8},{14,10},{1,13},{3,15... | collective-permute-start | bytes 98312 | tf_op jit(solution)/shard_map/ppermute | solution.py:136
  63.9 4.8 %collective-permute-start.9 = (bf16[128,128]{0,1:T(8,128)(2,1)S(1)}, bf16[128,128]{0,1:T(8,128)(2,1)S(1)}, u32[]{:S(2)}, u32[]{:S(2)}) collective-permute-start(bf16[128,128]{0,1:T(8,128)(2,1)S(1)} %get-tuple-element.20), channel_id=1, source_target_pairs={{0,10},{2,12},{4,14},{6,0},{8,2},{10,4},{12,6},{14,8},{1,11},{3,13... | collective-permute-start | bytes 98312 | tf_op jit(solution)/shard_map/ppermute | solution.py:136
